TPU v7x, 256 devices: a whole 4x4x8 slice. The times are simulated.
256 devices in a mesh: rows: 64 (over y, z, core), freq: 4 (over x).
Axes of the slice: x: 4, y: 4, z: 8, core: 2. Of those that a mesh axis runs over, the one named last changes fastest.
Arguments:
- snapshots: bfloat16 [1048576, 512], P('rows', 'freq'), may hold values from -60 to 60
- block_cols: int32 [8192, 3], P('rows'), may hold values from 0 to 8191, as said below
- mass_blocks: bfloat16 [8192, 3, 128, 128], P('rows'), may hold values from -2 to 2
- start_group: float32 [512, 32], P('freq'), may hold values from -6 to 6
- start_merge: float32 [64, 32], replicated, may hold values from -6 to 6
Outputs:
- modes: float32 [32, 1048576], P(None, ('rows', 'freq'))
Inputs may be any that keep to these rules, and one draw needn't show every extreme that they name: block_cols[b, 0] is b; the other entries lie within 2 of b, differ from b, and may repeat near the ends.
All inputs are finite; a program needn't handle non-finite values.
Results may differ from a plain program's by a relative error of at most 0.0003.
Values may be sent and summed in bfloat16 or wider, within the bound.
No kernel may reach another device: no remote copies, remote signals or barrier semaphores. Data moves between devices by JAX's collectives and lax.ppermute only.
A program may use at most 128 MiB of HBM per device.

v0:
```python
import jax
import jax.numpy as jnp
from jax import lax
from jax.sharding import PartitionSpec as P

HB = 2
POWER = 2


HIGHEST = lax.Precision.HIGHEST


def extended_2(block, sides, width):
    for axis, dim in sides:
        count = lax.axis_size(axis)
        forward = [(i, i + 1) for i in range(count - 1)]
        backward = [(target, source) for source, target in forward]
        low = lax.ppermute(
            lax.slice_in_dim(block, block.shape[dim] - width, None, axis=dim), axis, forward
        )
        high = lax.ppermute(lax.slice_in_dim(block, 0, width, axis=dim), axis, backward)
        block = jnp.concatenate([low, block, high], axis=dim)
    return block


def gathered_total(x, axis):
    return lax.all_gather(x, axis).sum(0)


def orthonormal(columns_block):
    inner_gram = jnp.dot(columns_block.T, columns_block, precision=HIGHEST)
    lower_factor = jnp.linalg.cholesky(inner_gram)
    return lax.linalg.triangular_solve(
        lower_factor, columns_block, left_side=False, lower=True, transpose_a=True
    )


def subspace(gram_matrix, start_block):
    current = start_block
    for repeat in range(POWER):
        current = orthonormal(jnp.dot(gram_matrix, current, precision=HIGHEST))
    return current


def coefficient_tree(full_gram, start_merge, rank_size, freq_count):
    identity_matrix = jnp.eye(freq_count * rank_size, dtype=jnp.float32)
    coefficients = [
        identity_matrix[:, group_id * rank_size : (group_id + 1) * rank_size]
        for group_id in range(freq_count)
    ]
    for section_index in range(freq_count.bit_length() - 1):
        merged = []
        for position in range(0, len(coefficients), 2):
            joined = jnp.concatenate([coefficients[position], coefficients[position + 1]], axis=1)
            pair_gram = jnp.dot(
                joined.T, jnp.dot(full_gram, joined, precision=HIGHEST), precision=HIGHEST
            )
            merged.append(jnp.dot(joined, subspace(pair_gram, start_merge), precision=HIGHEST))
        coefficients = merged
    return coefficients[0]


def own_share(full_rows, freq_count):
    share_width = full_rows.shape[1] // freq_count
    return lax.dynamic_slice_in_dim(full_rows, lax.axis_index("freq") * share_width, share_width, 1)


def shards(snapshots, block_cols, mass_blocks, start_group, start_merge):
    block_size = mass_blocks.shape[2]
    local_blocks = block_cols.shape[0]
    local_cols = snapshots.shape[1]
    total_rows = lax.axis_size("rows") * snapshots.shape[0]
    extended = extended_2(snapshots, (("rows", 0),), HB * block_size)
    tile_stack = extended.reshape(local_blocks + 2 * HB, block_size, local_cols)
    local_index = block_cols - lax.axis_index("rows") * local_blocks + HB
    picked = tile_stack[local_index]
    weighted = jnp.einsum("bkij,bkjc->bic", mass_blocks, picked, preferred_element_type=jnp.float32)
    weighted = weighted.reshape(local_blocks * block_size, local_cols)
    local_gram = jnp.dot(weighted.T, weighted, precision=HIGHEST)
    group_gram = gathered_total(local_gram, "rows") / total_rows
    weights = subspace(group_gram, start_group)
    modes = lax.dot_general(weights, weighted, (((0,), (1,)), ((), ())), precision=HIGHEST)
    rank_size = modes.shape[0]
    freq_count = lax.axis_size("freq")
    everyone = lax.all_gather(modes, "freq", axis=0, tiled=True)
    full_gram = (
        gathered_total(jnp.dot(everyone, everyone.T, precision=HIGHEST), "rows") / total_rows
    )
    combined = coefficient_tree(full_gram, start_merge, rank_size, freq_count)
    result = jnp.dot(combined.T, own_share(everyone, freq_count), precision=HIGHEST)
    return result


def solution(mesh):
    in_specs = (
        P("rows", "freq"),
        P("rows", None),
        P("rows", None, None, None),
        P("freq", None),
        P(),
    )
    out_specs = P(None, ("rows", "freq"))
    return jax.shard_map(shards, mesh=mesh, in_specs=in_specs, out_specs=out_specs, check_vma=False)
```

profile of v0, /device:TPU:32, one launch (start us, length us, event | category | flops | bytes accessed | tf_op | source)
XLA Modules:
  0.0 416.2 jit_solution(7248479484221727090)
XLA Ops:
  9.4 3.6 collective-permute-start.1
  14.9 10.8 %pad_maximum_fusion = bf16[16896,128]{1,0:T(8,128)(2,1)} fusion(bf16[256,128]{1,0:T(8,128)(2,1)S(1)} %collective-permute-done.1, bf16[16384,128]{1,0:T(8,128)(2,1)} %param.10, bf16[256,128]{1,0:T(8,128)(2,1)S(1)} %collective-permute-done), kind=kLoop, calls=%fused_computation.3 | loop fusion | flops 12976128 | bytes 8650752 | tf_op jit(solution)/shard_map/concatenate | solution.py:22
  25.7 13.6 %gather_fusion = bf16[384,128,128]{2,1,0:T(8,128)(2,1)} fusion(bf16[132,128,128]{2,1,0:T(8,128)(2,1)} %bitcast.157, s32[1024]{0:T(1024)S(1)} %pad_clamp_fusion), kind=kCustom, calls=%fused_computation | custom fusion | bytes 25167360 | tf_op jit(solution)/shard_map/gather | solution.py:76
  39.2 14.8 %fusion.90 = f32[128,128,128,1]{1,2,3,0:T(8,128)} fusion(bf16[128,3,128,128]{3,2,1,0:T(8,128)(2,1)} %param.12, bf16[128,3,128,128]{3,2,1,0:T(8,128)(2,1)} %bitcast.156), kind=kOutput, calls=%fused_computation.133 | convolution fusion | flops 1610612736 | bytes 33554432 | tf_op jit(solution)/shard_map/bkij,bkjc->bic/dot_general | solution.py:77
  54.0 17.6 %fusion.4 = f32[128,128]{1,0:T(8,128)} fusion(f32[128,128,128,1]{1,2,3,0:T(8,128)} %fusion.90), kind=kOutput, calls=%fused_computation.6 | convolution fusion | flops 3221225472 | bytes 8454144 | tf_op jit(solution)/shard_map/dot_general | solution.py:79
  71.7 82.5 %all-gather.8.cloned.1.call-done = f32[8192,128]{1,0:T(8,128)} async-done(((f32[128,128]{1,0:T(8,128)}), f32[8192,128]{1,0:T(8,128)}) %all-gather.8.cloned.1.call-update) | async-done | bytes 4194320 | tf_op jit(solution)/shard_map/all_gather | solution.py:27
  157.1 2.9 cholesky.134
  161.4 2.4 custom-call.14
  164.5 2.9 cholesky.145
  168.8 2.4 custom-call.15
  171.4 11.6 %fusion.76 = f32[32,16384]{1,0:T(8,128)} fusion(f32[128,32]{0,1:T(8,128)S(1)} %convolution_bitcast_fusion.6, f32[16384,128]{1,0:T(8,128)} %bitcast.155), kind=kOutput, calls=%fused_computation.119 | convolution fusion | flops 805306368 | bytes 10502144 | tf_op jit(solution)/shard_map/dot_general | solution.py:82
  183.1 83.7 %all-gather.6.cloned.1.call-done = f32[128,16384]{1,0:T(8,128)} async-done(((f32[32,16384]{1,0:T(8,128)}), f32[128,16384]{1,0:T(8,128)}) %all-gather.6.cloned.1.call-update) | async-done | bytes 8388624 | tf_op jit(solution)/shard_map/all_gather | solution.py:85
  266.9 11.1 %fusion.77 = f32[128,128]{1,0:T(8,128)} fusion(f32[128,16384]{1,0:T(8,128)} %all-gather.6.cloned.1.call-done), kind=kOutput, calls=%fused_computation.120 | convolution fusion | flops 3221225472 | bytes 8454144 | tf_op jit(solution)/shard_map/dot_general | solution.py:87
  278.0 79.4 %all-gather.10.cloned.1.call-done = f32[8192,128]{1,0:T(8,128)} async-done(((f32[128,128]{1,0:T(8,128)}), f32[8192,128]{1,0:T(8,128)}) %all-gather.10.cloned.1.call-update) | async-done | bytes 4194320 | tf_op jit(solution)/shard_map/all_gather | solution.py:27
  360.9 2.9 cholesky.156
  365.2 2.4 custom-call.16
  368.3 2.9 cholesky.167
  372.6 2.4 custom-call.17
  376.2 2.9 cholesky.178
  383.5 2.9 cholesky.189
  387.8 2.4 custom-call.19
  391.5 2.9 cholesky.200
  398.9 2.9 cholesky.211
  406.1 3.6 fusion.2
  (97 shorter events, 34.8 us)
Async XLA Ops:
  6.5 354.0 %copy-start = (f32[64,32]{0,1:T(8,128)S(1)}, f32[64,32]{0,1:T(8,128)}, u32[]{:S(2)}) copy-start(f32[64,32]{0,1:T(8,128)} %param.14) | copy-start | bytes 24580
  6.5 147.7 %all-gather.8.cloned.1.call-start = ((), (), s32[]{:S(2)}) async-start(), calls=%async_computation.1 | async-start | bytes 4259840 | tf_op jit(solution)/shard_map/all_gather | solution.py:27
  7.4 6.6 %collective-permute-start = (bf16[256,128]{1,0:T(8,128)(2,1)S(1)}, bf16[256,128]{1,0:T(8,128)(2,1)S(1)}, u32[]{:S(2)}, u32[]{:S(2)}) collective-permute-start(bf16[256,128]{1,0:T(8,128)(2,1)S(1)} %get-tuple-element.6), channel_id=1, source_target_pairs={{0,4},{4,8},{8,12},{12,16},{16,20},{20,24},{24,28},{28,32},{32,36}... | collective-permute-start | bytes 196616 | tf_op jit(solution)/shard_map/ppermute | solution.py:18
  9.4 5.5 %collective-permute-start.1 = (bf16[256,128]{1,0:T(8,128)(2,1)S(1)}, bf16[256,128]{1,0:T(8,128)(2,1)S(1)}, u32[]{:S(2)}, u32[]{:S(2)}) collective-permute-start(bf16[256,128]{1,0:T(8,128)(2,1)S(1)} %get-tuple-element.8), channel_id=1, source_target_pairs={{4,0},{8,4},{12,8},{16,12},{20,16},{24,20},{28,24},{32,28},{36,32}... | collective-permute-start | bytes 196616 | tf_op jit(solution)/shard_map/ppermute | solution.py:21
  54.0 102.6 %copy-start.1 = (f32[128,32]{0,1:T(8,128)S(1)}, f32[128,32]{0,1:T(8,128)}, u32[]{:S(2)}) copy-start(f32[128,32]{0,1:T(8,128)} %param.13) | copy-start | bytes 49156
  71.6 195.2 %all-gather.6.cloned.1.call-start = ((), (), s32[]{:S(2)}) async-start(), calls=%async_computation | async-start | bytes 10485760 | tf_op jit(solution)/shard_map/all_gather | solution.py:85
  183.1 174.3 %all-gather.10.cloned.1.call-start = ((), (), s32[]{:S(2)}) async-start(), calls=%async_computation.2 | async-start | bytes 4259840 | tf_op jit(solution)/shard_map/all_gather | solution.py:27
Sparse Core Ops, SparseCore 0:
  71.8 82.4 all-gather.7
  183.2 83.5 all-gather.5
  278.1 79.2 all-gather.9
where the time goes:
time: 419 us; the launch traced here: 416 us
  waiting for transfers between devices  247 us (59%)
  other arithmetic  69.9 us (17%)
  matrix products  65.3 us (16%)
  local copies, waits for them, and re-layouts  15.3 us (4%)
  between operations  13.6 us (3%)
  starting transfers between devices  5.65 us (1%)
    all_gather x2, waiting for transfers between devices, gathered_total(): return lax.all_gather(x, axis).sum(0)  162 us
    all_gather x1, waiting for transfers between devices, shards(): everyone = lax.all_gather(modes, 'freq', axis=0, tiled=True)  83.7 us
    another operation x24, other arithmetic, orthonormal(): lower_factor = jnp.linalg.cholesky(inner_gram)  28.8 us
    another operation x16, other arithmetic, orthonormal(): lax.linalg.triangular_solve(lower_factor, columns_block, left_side=False,...  24.7 us
    dot_general x1, matrix products, shards(): local_gram = jnp.dot(weighted.T, weighted, precision=HIGHEST)  17.6 us
    dot_general x1, matrix products, shards(): jnp.einsum('bkij,bkjc->bic', mass_blocks, picked, preferred_element_type=...  14.8 us
    gather x1, local copies, waits for them, and re-layouts, shards(): picked = tile_stack[local_index]  13.6 us
    dot_general x1, matrix products, shards(): lax.dot_general(weights, weighted, (((0,), (1,)), ((), ())), precision=HI...  11.6 us
  transfers between devices with their start and end apart: 5, of which 4 were waited for; matrix products, arithmetic and copies ran while one was open for 0% of the time, Pallas kernels for 0%

commit v1 on v0

--- a/solution.py
+++ b/solution.py
@@ -23,10 +23,6 @@
     return block
 
 
-def gathered_total(x, axis):
-    return lax.all_gather(x, axis).sum(0)
-
-
 def orthonormal(columns_block):
     inner_gram = jnp.dot(columns_block.T, columns_block, precision=HIGHEST)
     lower_factor = jnp.linalg.cholesky(inner_gram)
@@ -43,12 +39,19 @@
 
 
 def coefficient_tree(full_gram, start_merge, rank_size, freq_count):
-    identity_matrix = jnp.eye(freq_count * rank_size, dtype=jnp.float32)
-    coefficients = [
-        identity_matrix[:, group_id * rank_size : (group_id + 1) * rank_size]
-        for group_id in range(freq_count)
-    ]
-    for section_index in range(freq_count.bit_length() - 1):
+    pairs = freq_count // 2
+    width = 2 * rank_size
+    blocks = jnp.stack(
+        [full_gram[p * width : (p + 1) * width, p * width : (p + 1) * width] for p in range(pairs)]
+    )
+    pair_weights = jax.vmap(subspace, in_axes=(0, None))(blocks, start_merge)
+    zero = jnp.zeros((width, rank_size), jnp.float32)
+    coefficients = []
+    for p in range(pairs):
+        parts = [zero] * pairs
+        parts[p] = pair_weights[p]
+        coefficients.append(jnp.concatenate(parts, axis=0))
+    while len(coefficients) > 1:
         merged = []
         for position in range(0, len(coefficients), 2):
             joined = jnp.concatenate([coefficients[position], coefficients[position + 1]], axis=1)
@@ -58,11 +61,6 @@
             merged.append(jnp.dot(joined, subspace(pair_gram, start_merge), precision=HIGHEST))
         coefficients = merged
     return coefficients[0]
-
-
-def own_share(full_rows, freq_count):
-    share_width = full_rows.shape[1] // freq_count
-    return lax.dynamic_slice_in_dim(full_rows, lax.axis_index("freq") * share_width, share_width, 1)
 
 
 def shards(snapshots, block_cols, mass_blocks, start_group, start_merge):
@@ -77,17 +75,17 @@
     weighted = jnp.einsum("bkij,bkjc->bic", mass_blocks, picked, preferred_element_type=jnp.float32)
     weighted = weighted.reshape(local_blocks * block_size, local_cols)
     local_gram = jnp.dot(weighted.T, weighted, precision=HIGHEST)
-    group_gram = gathered_total(local_gram, "rows") / total_rows
+    group_gram = lax.psum(local_gram, "rows") / total_rows
     weights = subspace(group_gram, start_group)
     modes = lax.dot_general(weights, weighted, (((0,), (1,)), ((), ())), precision=HIGHEST)
     rank_size = modes.shape[0]
     freq_count = lax.axis_size("freq")
-    everyone = lax.all_gather(modes, "freq", axis=0, tiled=True)
+    quarter = lax.all_to_all(modes, "freq", 1, 0, tiled=True)
     full_gram = (
-        gathered_total(jnp.dot(everyone, everyone.T, precision=HIGHEST), "rows") / total_rows
+        lax.psum(jnp.dot(quarter, quarter.T, precision=HIGHEST), ("rows", "freq")) / total_rows
     )
     combined = coefficient_tree(full_gram, start_merge, rank_size, freq_count)
-    result = jnp.dot(combined.T, own_share(everyone, freq_count), precision=HIGHEST)
+    result = jnp.dot(combined.T, quarter, precision=HIGHEST)
     return result
 
 

time: 419 us -> 597 us (1.42)
  waiting for transfers between devices: 247 us -> 437 us
  matrix products: 65.3 us -> 56.6 us
  other arithmetic: 69.9 us -> 61.4 us
    psum x0 -> x2, waiting for transfers between devices: none -> 409 us  [the longest x1 236 us: shards(): lax.psum(jnp.dot(quarter, quarter.T, precision=HIGHEST), ('rows', 'freq'))]
    all_gather x3 -> x0, waiting for transfers between devices: 246 us -> none  [the longest x2 162 us: gathered_total(): return lax.all_gather(x, axis).sum(0)]
    all_to_all x0 -> x1, waiting for transfers between devices: none -> 27.5 us  [shards(): quarter = lax.all_to_all(modes, 'freq', 1, 0, tiled=True)]
    dot_general x2, matrix products: 14.7 us -> 4.4 us  [the longest x1 2.42 us: shards(): jnp.dot(quarter, quarter.T, precision=HIGHEST)]
    another operation x16 -> x13, other arithmetic: 24.7 us -> 22.3 us  [orthonormal(): lax.linalg.triangular_solve(lower_factor, columns_block, left_side=False,...]
    another operation x24 -> x19, other arithmetic: 28.8 us -> 26.7 us  [orthonormal(): lower_factor = jnp.linalg.cholesky(inner_gram)]
where the time goes in v1:
time: 597 us; the launch traced here: 594 us
  waiting for transfers between devices  437 us (73%)
  other arithmetic  61.4 us (10%)
  matrix products  56.6 us (9%)
  local copies, waits for them, and re-layouts  15.3 us (3%)
  between operations  13.7 us (2%)
  starting transfers between devices  9.81 us (2%)
    psum x1, waiting for transfers between devices, shards(): lax.psum(jnp.dot(quarter, quarter.T, precision=HIGHEST), ('rows', 'freq'))  236 us
    psum x1, waiting for transfers between devices, shards(): group_gram = lax.psum(local_gram, 'rows') / total_rows  173 us
    all_to_all x1, waiting for transfers between devices, shards(): quarter = lax.all_to_all(modes, 'freq', 1, 0, tiled=True)  27.5 us
    another operation x19, other arithmetic, orthonormal(): lower_factor = jnp.linalg.cholesky(inner_gram)  26.7 us
    another operation x13, other arithmetic, orthonormal(): lax.linalg.triangular_solve(lower_factor, columns_block, left_side=False,...  22.3 us
    dot_general x1, matrix products, shards(): local_gram = jnp.dot(weighted.T, weighted, precision=HIGHEST)  17.6 us
    dot_general x1, matrix products, shards(): jnp.einsum('bkij,bkjc->bic', mass_blocks, picked, preferred_element_type=...  14.8 us
    gather x1, local copies, waits for them, and re-layouts, shards(): picked = tile_stack[local_index]  13.6 us
  transfers between devices with their start and end apart: 5, of which 4 were waited for; matrix products, arithmetic and copies ran while one was open for 0% of the time, Pallas kernels for 0%

profile of v1, /device:TPU:32, one launch (start us, length us, event | category | flops | bytes accessed | tf_op | source)
XLA Modules:
  0.0 594.3 jit_solution(17205891390755514347)
XLA Ops:
  9.4 3.6 collective-permute-start.1
  14.9 10.8 %pad_maximum_fusion = bf16[16896,128]{1,0:T(8,128)(2,1)} fusion(bf16[256,128]{1,0:T(8,128)(2,1)S(1)} %collective-permute-done.1, bf16[16384,128]{1,0:T(8,128)(2,1)} %param.13, bf16[256,128]{1,0:T(8,128)(2,1)S(1)} %collective-permute-done), kind=kLoop, calls=%fused_computation.3 | loop fusion | flops 12976128 | bytes 8650752 | tf_op jit(solution)/shard_map/concatenate | solution.py:22
  25.7 13.6 %gather_fusion = bf16[384,128,128]{2,1,0:T(8,128)(2,1)} fusion(bf16[132,128,128]{2,1,0:T(8,128)(2,1)} %bitcast.133, s32[1024]{0:T(1024)S(1)} %pad_clamp_fusion), kind=kCustom, calls=%fused_computation | custom fusion | bytes 25167360 | tf_op jit(solution)/shard_map/gather | solution.py:74
  39.2 14.8 %fusion.62 = f32[128,128,128,1]{1,2,3,0:T(8,128)} fusion(bf16[128,3,128,128]{3,2,1,0:T(8,128)(2,1)} %param.15, bf16[128,3,128,128]{3,2,1,0:T(8,128)(2,1)} %bitcast.132), kind=kOutput, calls=%fused_computation.103 | convolution fusion | flops 1610612736 | bytes 33554432 | tf_op jit(solution)/shard_map/bkij,bkjc->bic/dot_general | solution.py:75
  54.0 17.6 %fusion.2 = f32[128,128]{1,0:T(8,128)} fusion(f32[128,128,128,1]{1,2,3,0:T(8,128)} %fusion.62), kind=kOutput, calls=%fused_computation.4 | convolution fusion | flops 3221225472 | bytes 8454144 | tf_op jit(solution)/shard_map/dot_general | solution.py:77
  71.6 173.5 %all-reduce.5.cloned.1.call-done = f32[128,128]{1,0:T(8,128)} async-done(((f32[128,128]{1,0:T(8,128)}), f32[128,128]{1,0:T(8,128)}) %all-reduce.5.cloned.1.call-update) | async-done | bytes 65552 | tf_op jit(solution)/shard_map/psum | solution.py:78
  246.4 2.9 cholesky.117
  250.7 2.4 custom-call.18
  254.7 2.9 cholesky.128
  258.9 2.4 custom-call.19
  261.6 13.0 %fusion.53 = f32[32,4,4096]{2,0,1:T(8,128)} fusion(f32[128,32,1]{0,1,2:T(8,128)S(1)} %convolution_bitcast_fusion.4, f32[4,4096,128]{2,1,0:T(8,128)} %bitcast.131), kind=kOutput, calls=%fused_computation.94 | convolution fusion | flops 805306368 | bytes 10502144 | tf_op jit(solution)/shard_map/dot_general | solution.py:80
  274.6 4.2 all-to-all-start
  278.8 27.5 %all-to-all-done = f32[32,4,4096]{2,0,1:T(8,128)S(1)} async-done(((f32[32,4,4096]{2,0,1:T(8,128)}), f32[32,4,4096]{2,0,1:T(8,128)S(1)}, u32[]{:S(2)}, u32[]{:S(2)}) %all-to-all-start) | async-done | bytes 2097184 | tf_op jit(solution)/shard_map/all_to_all | solution.py:83
  306.3 2.4 fusion.54
  308.8 235.5 %all-reduce.7.cloned.1.call-done = f32[128,128]{1,0:T(8,128)} async-done(((f32[128,128]{1,0:T(8,128)}), f32[128,128]{1,0:T(8,128)}) %all-reduce.7.cloned.1.call-update) | async-done | bytes 65552 | tf_op jit(solution)/shard_map/psum | solution.py:85
  545.8 6.1 %custom-call.20 = f32[2,32,32]{2,1,0:T(8,128)S(1)} custom-call(f32[2,32,32]{2,1,0:T(8,128)S(1)} %fusion.14), custom_call_target="Cholesky" | custom-call | tf_op jit(solution)/shard_map/vmap(jit(cholesky))/cholesky | solution.py:28
  552.2 4.9 custom-call.21
  557.9 5.9 custom-call.22
  564.0 4.9 custom-call.23
  570.9 2.9 cholesky.161
  575.2 2.4 custom-call.24
  578.3 2.9 cholesky.172
  582.5 2.4 custom-call.25
  585.4 2.0 fusion.61
  (72 shorter events, 18.8 us)
Async XLA Ops:
  6.5 538.7 %copy-start = (f32[64,32]{0,1:T(8,128)S(1)}, f32[64,32]{0,1:T(8,128)}, u32[]{:S(2)}) copy-start(f32[64,32]{0,1:T(8,128)} %param.17) | copy-start | bytes 24580
  6.5 238.6 %all-reduce.5.cloned.1.call-start = ((), (), s32[]{:S(2)}) async-start(), calls=%async_computation.1 | async-start | bytes 131072 | tf_op jit(solution)/shard_map/psum | solution.py:78
  7.4 6.6 %collective-permute-start = (bf16[256,128]{1,0:T(8,128)(2,1)S(1)}, bf16[256,128]{1,0:T(8,128)(2,1)S(1)}, u32[]{:S(2)}, u32[]{:S(2)}) collective-permute-start(bf16[256,128]{1,0:T(8,128)(2,1)S(1)} %get-tuple-element.6), channel_id=1, source_target_pairs={{0,4},{4,8},{8,12},{12,16},{16,20},{20,24},{24,28},{28,32},{32,36}... | collective-permute-start | bytes 196616 | tf_op jit(solution)/shard_map/ppermute | solution.py:18
  9.4 5.5 collective-permute-start.1
  54.0 191.1 %copy-start.1 = (f32[128,32]{0,1:T(8,128)S(1)}, f32[128,32]{0,1:T(8,128)}, u32[]{:S(2)}) copy-start(f32[128,32]{0,1:T(8,128)} %param.16) | copy-start | bytes 49156
  274.6 31.8 %all-to-all-start = ((f32[32,4,4096]{2,0,1:T(8,128)}), f32[32,4,4096]{2,0,1:T(8,128)S(1)}, u32[]{:S(2)}, u32[]{:S(2)}) async-start(f32[32,4,4096]{2,0,1:T(8,128)} %fusion.53), calls=%async_computation | async-start | bytes 4194304 | tf_op jit(solution)/shard_map/all_to_all | solution.py:83
  278.8 265.5 %all-reduce.7.cloned.1.call-start = ((), (), s32[]{:S(2)}) async-start(), calls=%async_computation.2 | async-start | bytes 131072 | tf_op jit(solution)/shard_map/psum | solution.py:85
Sparse Core Ops, SparseCore 0:
  71.8 173.2 all-reduce.4
  308.9 235.3 all-reduce.6
